TPU v7x, 512 devices: a whole 4x8x8 slice. The times are simulated.
512 devices in a mesh: ctx: 32 (over y, x), fsdp: 16 (over z, core).
Axes of the slice: x: 4, y: 8, z: 8, core: 2. Of those that a mesh axis runs over, the one named last changes fastest.
Arguments:
- tokens: bfloat16 [131072, 4096], P(('ctx', 'fsdp')), may hold values from -48 to 48
- query_weight: bfloat16 [4096, 512], P('fsdp'), may hold values from -0.09375 to 0.09375
- key_weight: bfloat16 [4096, 128], P('fsdp'), may hold values from -0.09375 to 0.09375
- value_weight: bfloat16 [4096, 128], P('fsdp'), may hold values from -0.09375 to 0.09375
- chosen: int32 [256, 2], replicated, may hold values from 0 to 253, as said below
Outputs:
- attended: bfloat16 [131072, 512], P(('ctx', 'fsdp'))
Inputs may be any that keep to these rules, and one draw needn't show every extreme that they name: `chosen`: for query block q >= 3 both entries are distinct and below q - 1; block 2 names block 0 twice; blocks 0 and 1 name 0 twice, which selects nothing. The last block always selects block 253.
All inputs are finite; a program needn't handle non-finite values.
Results may differ from a plain program's by a relative error of at most 0.0065.
The roundings to bfloat16 on the way count: a program that leaves them out, or rounds other values in their place, can miss the bound.
Values may be sent and summed in bfloat16 or wider, within the bound.
No kernel may reach another device: no remote copies, remote signals or barrier semaphores. Data moves between devices by JAX's collectives and lax.ppermute only.
A program may use at most 64 MiB of HBM per device.

v0:
```python
import jax
import jax.numpy as jnp
from jax import lax
from jax.sharding import PartitionSpec as P

QH = 4


def from_behind(array, axis, by):
    peers = lax.axis_size(axis)
    pairs = [(i, i + by) for i in range(peers) if 0 <= i + by < peers]
    return lax.ppermute(array, axis, pairs)


def project_rows(tokens, pieces):
    return tuple(
        (
            jnp.dot(tokens, weight_piece, preferred_element_type=jnp.float32)
            for weight_piece in pieces
        )
    )


def per_device(tokens, query_weight, key_weight, value_weight, chosen):
    token_rows = tokens.shape[0]
    head_width = key_weight.shape[1]
    pair_width = 2 * head_width
    lane_count = lax.axis_size("fsdp")
    lane_index = lax.axis_index("fsdp")
    group_index = lax.axis_index("ctx")
    blocks_group = lane_count // 2
    my_block = group_index * blocks_group + lane_index // 2
    global_index = group_index * lane_count + lane_index
    projected = project_rows(
        tokens,
        (
            lax.all_gather(query_weight, "fsdp", axis=0, tiled=True),
            lax.all_gather(key_weight, "fsdp", axis=0, tiled=True),
            lax.all_gather(value_weight, "fsdp", axis=0, tiled=True),
        ),
    )
    queries = projected[0].astype(jnp.bfloat16).reshape(token_rows, QH, head_width)
    key_value = jnp.concatenate(
        [projected[1].astype(jnp.bfloat16), projected[2].astype(jnp.bfloat16)], axis=1
    )
    before_pair = from_behind(key_value, ("ctx", "fsdp"), 1)
    own_block = jnp.concatenate([before_pair, key_value], axis=0)
    candidates = lax.all_gather(key_value, "ctx", axis=0, tiled=True).reshape(
        -1, token_rows, pair_width
    )
    wanted = jnp.repeat(
        lax.dynamic_slice_in_dim(chosen, group_index * blocks_group, blocks_group, 0), 2, axis=0
    )
    dest_block = group_index * blocks_group + jnp.arange(lane_count, dtype=jnp.int32) // 2
    live_first = wanted[:, 0] < dest_block - 1
    live_second = (wanted[:, 1] < dest_block - 1) & (wanted[:, 1] != wanted[:, 0])
    mine = lax.dynamic_index_in_dim(chosen, my_block, 0, keepdims=False)
    sending = jnp.stack([live_first, live_second], axis=1) & (
        wanted % blocks_group == lane_index // 2
    )
    outgoing = jnp.take(candidates, (wanted // blocks_group).reshape(-1), axis=0)
    outgoing = outgoing.reshape(lane_count, 2, token_rows, pair_width)
    outgoing = jnp.where(sending[:, :, None, None], outgoing, jnp.zeros_like(outgoing))
    incoming = lax.all_to_all(outgoing, "fsdp", split_axis=0, concat_axis=0, tiled=True)

    def assemble(which):
        place = mine[which] % blocks_group * 2
        column_slot = incoming[:, which]
        return jnp.concatenate(
            [
                lax.dynamic_index_in_dim(column_slot, place, 0, keepdims=False),
                lax.dynamic_index_in_dim(column_slot, place + 1, 0, keepdims=False),
            ],
            axis=0,
        )

    block_first = assemble(0)
    block_second = assemble(1)
    key_rows = jnp.concatenate(
        [own_block[:, :head_width], block_first[:, :head_width], block_second[:, :head_width]],
        axis=0,
    )
    value_rows = jnp.concatenate(
        [own_block[:, head_width:], block_first[:, head_width:], block_second[:, head_width:]],
        axis=0,
    )
    scores = jnp.einsum(
        "qhd,kd->hqk", queries, key_rows, preferred_element_type=jnp.float32
    ) * head_width ** (-0.5)
    window_rows = own_block.shape[0]
    pick_rows = block_first.shape[0]
    row_index = jnp.arange(token_rows, dtype=jnp.int32)
    column = jnp.arange(window_rows, dtype=jnp.int32)
    causal = (column[None, :] <= row_index[:, None] + token_rows) & (
        (column[None, :] >= token_rows) | (global_index > 0)
    )
    first_ok = mine[0] < my_block - 1
    second_ok = (mine[1] < my_block - 1) & (mine[1] != mine[0])
    visible = jnp.concatenate(
        [
            causal,
            jnp.broadcast_to(first_ok, (token_rows, pick_rows)),
            jnp.broadcast_to(second_ok, (token_rows, pick_rows)),
        ],
        axis=1,
    )
    scores = jnp.where(visible[None], scores, -jnp.inf)
    highest = jnp.max(scores, axis=2, keepdims=True)
    probs = jnp.exp(scores - highest)
    denominator = jnp.sum(probs, axis=2, keepdims=True)
    mixed = (
        jnp.einsum(
            "hqk,kd->hqd",
            probs.astype(jnp.bfloat16),
            value_rows,
            preferred_element_type=jnp.float32,
        )
        / denominator
    )
    return jnp.transpose(mixed, (1, 0, 2)).reshape(token_rows, -1).astype(jnp.bfloat16)


def solution(mesh):
    return jax.shard_map(
        per_device,
        mesh=mesh,
        in_specs=(P(("ctx", "fsdp"), None), P("fsdp", None), P("fsdp", None), P("fsdp", None), P()),
        out_specs=P(("ctx", "fsdp"), None),
        check_vma=False,
    )
```

profile of v0, /device:TPU:6, one launch (start us, length us, event | category | flops | bytes accessed | tf_op | source)
XLA Modules:
  0.0 340.2 jit_solution(2382489390191044968)
XLA Ops:
  6.5 0.0 copy-start
  6.5 0.0 copy-start.2
  6.5 0.0 all-gather.7.cloned.1.call-start
  6.5 0.7 all-gather.7.cloned.1.call-update
  7.3 0.0 all-gather.5.cloned.1.call-start
  7.3 0.7 all-gather.5.cloned.1.call-update
  8.0 0.0 all-gather.9.cloned.1.call-start
  8.1 48.0 %all-gather.7.cloned.1.call-done = bf16[4096,128]{1,0:T(8,128)(2,1)} async-done(((bf16[256,128]{1,0:T(8,128)(2,1)}), bf16[4096,128]{1,0:T(8,128)(2,1)}) %all-gather.7.cloned.1.call-update) | async-done | bytes 1048592 | tf_op jit(solution)/shard_map/all_gather | solution.py:39
  56.1 0.0 copy-done
  56.1 2.1 convolution_convert_fusion.1
  58.1 40.2 %all-gather.5.cloned.1.call-done = bf16[4096,128]{1,0:T(8,128)(2,1)} async-done(((bf16[256,128]{1,0:T(8,128)(2,1)}), bf16[4096,128]{1,0:T(8,128)(2,1)}) %all-gather.5.cloned.1.call-update) | async-done | bytes 1048592 | tf_op jit(solution)/shard_map/all_gather | solution.py:38
  98.3 2.1 convolution_convert_fusion.2
  100.3 0.7 pad_maximum_fusion.2
  101.0 0.0 all-gather.9.cloned.1.call-update
  101.0 0.0 all-gather.11.cloned.1.call-start
  101.1 0.5 all-gather.11.cloned.1.call-update
  101.6 0.0 copy-done.2
  101.6 0.1 constant_dynamic-slice_fusion
  101.7 0.1 copy.15
  101.8 0.1 reshape.211
  101.9 0.1 copy.27
  102.0 0.1 copy.17
  102.1 0.1 copy.18
  102.2 86.4 %all-gather.9.cloned.1.call-done = bf16[8192,256]{0,1:T(8,128)(2,1)} async-done(((bf16[256,256]{0,1:T(8,128)(2,1)}), bf16[8192,256]{0,1:T(8,128)(2,1)}) %all-gather.9.cloned.1.call-update) | async-done | bytes 4194320 | tf_op jit(solution)/shard_map/all_gather | solution.py:48
  188.6 6.4 %copy.28 = bf16[8192,256]{1,0:T(8,128)(2,1)} copy(bf16[8192,256]{0,1:T(8,128)(2,1)} %all-gather.9.cloned.1.call-done) | data formatting | bytes 8388608 | tf_op jit(solution)/shard_map/reshape | solution.py:48
  195.0 5.0 %gather_fusion = bf16[32,256,256]{2,1,0:T(8,128)(2,1)} fusion(bf16[32,256,256]{2,1,0:T(8,128)(2,1)} %bitcast.59, s32[1024]{0:T(1024)S(1)} %pad_clamp_fusion), kind=kCustom, calls=%fused_computation | custom fusion | bytes 8388736 | tf_op jit(solution)/shard_map/jit(_take)/gather | solution.py:61
  200.0 6.4 %copy.20 = bf16[16,2,256,256]{2,3,1,0:T(8,128)(2,1)} copy(bf16[16,2,256,256]{3,2,1,0:T(8,128)(2,1)} %bitcast.60) | data formatting | bytes 8388608 | tf_op jit(solution)/shard_map/jit(_take)/gather | solution.py:61
  206.4 4.7 %select_select_fusion = bf16[16,2,256,256]{2,3,1,0:T(8,128)(2,1)} fusion(bf16[16,2,256,256]{2,3,1,0:T(8,128)(2,1)} %copy.20, pred[16,2]{1,0:T(8,128)(4,1)S(1)} %copy.18, pred[16,2]{1,0:T(8,128)(4,1)S(1)} %copy.17), kind=kLoop, calls=%fused_computation.6 | loop fusion | flops 4194304 | bytes 8388672 | tf_op jit(solution)/shard_map/jit(_where)/select_n | solution.py:63
  211.1 0.0 copy-start.1
  211.1 7.7 %all-to-all-start = ((bf16[16,2,256,256]{2,3,1,0:T(8,128)(2,1)}), bf16[16,2,256,256]{2,3,1,0:T(8,128)(2,1)}, u32[]{:S(2)}, u32[]{:S(2)}) async-start(bf16[16,2,256,256]{2,3,1,0:T(8,128)(2,1)} %select_select_fusion), calls=%async_computation | async-start | bytes 8388608 | tf_op jit(solution)/shard_map/all_to_all | solution.py:64
  218.9 0.1 constant_dynamic-slice_fusion.1
  219.0 0.6 fusion.44
  222.2 0.1 fusion.16
  222.3 0.0 copy-done.1
  222.3 2.3 collective-permute-start
  224.6 1.4 add_add_fusion
  229.9 92.4 %collective-permute-done = bf16[256,256]{0,1:T(8,128)(2,1)S(1)} collective-permute-done((bf16[256,256]{0,1:T(8,128)(2,1)S(1)}, bf16[256,256]{0,1:T(8,128)(2,1)S(1)}, u32[]{:S(2)}, u32[]{:S(2)}) %collective-permute-start) | collective-permute-done | bytes 131104 | tf_op jit(solution)/shard_map/ppermute | solution.py:12
  322.3 0.0 all-gather.11.cloned.1.call-done
  322.3 3.4 %fusion.9 = bf16[32,4,8,128]{3,2,1,0:T(8,128)(2,1)S(1)} fusion(bf16[256,4096]{1,0:T(8,128)(2,1)S(1)} %copy-done, bf16[4096,512]{1,0:T(8,128)(2,1)} %all-gather.11.cloned.1.call-done), kind=kOutput, calls=%fused_computation.12 | convolution fusion | flops 1073872896 | bytes 6553600 | tf_op jit(solution)/shard_map/dot_general | solution.py:18
  325.8 0.0 all-to-all-done
  325.8 2.7 fusion.42
  328.5 1.2 fusion.2
  329.7 1.3 fusion
  331.0 1.8 fusion.13
  332.8 0.8 copy.24
  (16 shorter events, 0.2 us)
Async XLA Ops:
  6.5 49.5 %copy-start = (bf16[256,4096]{1,0:T(8,128)(2,1)S(1)}, bf16[256,4096]{1,0:T(8,128)(2,1)}, u32[]{:S(2)}) copy-start(bf16[256,4096]{1,0:T(8,128)(2,1)} %param.5) | copy-start | bytes 6291460
  6.5 95.1 %copy-start.2 = (s32[256,2]{0,1:T(2,128)S(1)}, s32[256,2]{0,1:T(2,128)}, u32[]{:S(2)}) copy-start(s32[256,2]{0,1:T(2,128)} %param.9) | copy-start | bytes 6148
  6.5 49.5 %all-gather.7.cloned.1.call-start = ((), (), s32[]{:S(2)}) async-start(), calls=%async_computation.2 | async-start | bytes 1114112 | tf_op jit(solution)/shard_map/all_gather | solution.py:39
  7.3 91.0 %all-gather.5.cloned.1.call-start = ((), (), s32[]{:S(2)}) async-start(), calls=%async_computation.1 | async-start | bytes 1114112 | tf_op jit(solution)/shard_map/all_gather | solution.py:38
  8.0 180.6 %all-gather.9.cloned.1.call-start = ((), (), s32[]{:S(2)}) async-start(), calls=%async_computation.3 | async-start | bytes 4325376 | tf_op jit(solution)/shard_map/all_gather | solution.py:48
  101.0 221.3 %all-gather.11.cloned.1.call-start = ((), (), s32[]{:S(2)}) async-start(), calls=%async_computation.4 | async-start | bytes 4456448 | tf_op jit(solution)/shard_map/all_gather | solution.py:37
  211.1 11.2 %copy-start.1 = (bf16[256,256]{0,1:T(8,128)(2,1)S(1)}, bf16[256,256]{0,1:T(8,128)(2,1)}, u32[]{:S(2)}) copy-start(bf16[256,256]{0,1:T(8,128)(2,1)} %pad_maximum_fusion.2) | copy-start | bytes 393220
  211.1 114.6 %all-to-all-start = ((bf16[16,2,256,256]{2,3,1,0:T(8,128)(2,1)}), bf16[16,2,256,256]{2,3,1,0:T(8,128)(2,1)}, u32[]{:S(2)}, u32[]{:S(2)}) async-start(bf16[16,2,256,256]{2,3,1,0:T(8,128)(2,1)} %select_select_fusion), calls=%async_computation | async-start | bytes 8388608 | tf_op jit(solution)/shard_map/all_to_all | solution.py:64
  222.3 99.9 %collective-permute-start = (bf16[256,256]{0,1:T(8,128)(2,1)S(1)}, bf16[256,256]{0,1:T(8,128)(2,1)S(1)}, u32[]{:S(2)}, u32[]{:S(2)}) collective-permute-start(bf16[256,256]{0,1:T(8,128)(2,1)S(1)} %copy-done.1), channel_id=1, source_target_pairs={{0,1},{1,2},{2,3},{3,4},{4,5},{5,6},{6,7},{7,8},{8,9},{9,10},{10,1... | collective-permute-start | bytes 393224 | tf_op jit(solution)/shard_map/ppermute | solution.py:12
Sparse Core Ops, SparseCore 0:
  9.5 46.5 all-gather.6
  58.2 40.0 all-gather.4
  101.3 87.2 all-gather.8
  190.6 80.9 all-gather.10
where the time goes:
time: 341 us; the launch traced here: 340 us
  waiting for transfers between devices  269 us (79%)
  local copies, waits for them, and re-layouts  22.6 us (7%)
  between operations  19.7 us (6%)
  matrix products  10.5 us (3%)
  starting transfers between devices  10.1 us (3%)
  other arithmetic  8.39 us (2%)
    ppermute x1, waiting for transfers between devices, from_behind(): return lax.ppermute(array, axis, pairs)  92.4 us
    all_gather x1, waiting for transfers between devices, per_device(): lax.all_gather(key_value, 'ctx', axis=0, tiled=True)  86.4 us
    all_gather x1, waiting for transfers between devices, per_device(): lax.all_gather(value_weight, 'fsdp', axis=0, tiled=True)  48 us
    all_gather x1, waiting for transfers between devices, per_device(): lax.all_gather(key_weight, 'fsdp', axis=0, tiled=True)  40.2 us
    gather x2, local copies, waits for them, and re-layouts, per_device(): jnp.take(candidates, (wanted // blocks_group).reshape(-1), axis=0)  11.4 us
    all_to_all x1, starting transfers between devices, per_device(): lax.all_to_all(outgoing, 'fsdp', split_axis=0, concat_axis=0, tiled=True)  7.75 us
    dot_general x3, matrix products, project_rows(): jnp.dot(tokens, weight_piece, preferred_element_type=jnp.float32)  7.53 us
  transfers between devices with their start and end apart: 6, of which 4 were waited for; matrix products, arithmetic and copies ran while one was open for 9% of the time, Pallas kernels for 0%

commit v1 on v0

--- a/solution.py
+++ b/solution.py
@@ -4,6 +4,11 @@
 from jax.sharding import PartitionSpec as P
 
 QH = 4
+
+
+def gather_from_all(shard, axis, dim):
+    copies = jnp.concatenate([shard] * lax.axis_size(axis), axis=dim)
+    return lax.all_to_all(copies, axis, dim, dim, tiled=True)
 
 
 def from_behind(array, axis, by):
@@ -35,7 +40,7 @@
         tokens,
         (
             lax.all_gather(query_weight, "fsdp", axis=0, tiled=True),
-            lax.all_gather(key_weight, "fsdp", axis=0, tiled=True),
+            gather_from_all(key_weight, "fsdp", 0),
             lax.all_gather(value_weight, "fsdp", axis=0, tiled=True),
         ),
     )

time: 341 us -> 323 us (0.947)
  waiting for transfers between devices: 269 us -> 226 us
  local copies, waits for them, and re-layouts: 22.6 us -> 37.4 us
  starting transfers between devices: 10.1 us -> 20.7 us
    all_gather x1 -> x0, waiting for transfers between devices: 40.2 us -> none  [per_device(): lax.all_gather(key_weight, 'fsdp', axis=0, tiled=True)]
    all_gather x1, waiting for transfers between devices: 48 us -> 20 us  [per_device(): lax.all_gather(value_weight, 'fsdp', axis=0, tiled=True)]
    all_to_all x0 -> x1, waiting for transfers between devices: none -> 26.5 us  [gather_from_all(): return lax.all_to_all(copies, axis, dim, dim, tiled=True)]
    unnamed x6 -> x23, local copies, waits for them, and re-layouts: 0.01 us -> 13.9 us
    all_to_all x0 -> x1, starting transfers between devices: none -> 10.6 us  [gather_from_all(): return lax.all_to_all(copies, axis, dim, dim, tiled=True)]
where the time goes in v1:
time: 323 us; the launch traced here: 322 us
  waiting for transfers between devices  226 us (70%)
  local copies, waits for them, and re-layouts  37.4 us (12%)
  starting transfers between devices  20.7 us (6%)
  between operations  19.8 us (6%)
  matrix products  9.26 us (3%)
  other arithmetic  8.39 us (3%)
    ppermute x1, waiting for transfers between devices, from_behind(): return lax.ppermute(array, axis, pairs)  92.5 us
    all_gather x1, waiting for transfers between devices, per_device(): lax.all_gather(key_value, 'ctx', axis=0, tiled=True)  86 us
    all_to_all x1, waiting for transfers between devices, gather_from_all(): return lax.all_to_all(copies, axis, dim, dim, tiled=True)  26.5 us
    all_gather x1, waiting for transfers between devices, per_device(): lax.all_gather(value_weight, 'fsdp', axis=0, tiled=True)  20 us
    unnamed x23, local copies, waits for them, and re-layouts  13.9 us
    gather x2, local copies, waits for them, and re-layouts, per_device(): jnp.take(candidates, (wanted // blocks_group).reshape(-1), axis=0)  11.4 us
    all_to_all x1, starting transfers between devices, gather_from_all(): return lax.all_to_all(copies, axis, dim, dim, tiled=True)  10.6 us
    all_to_all x1, starting transfers between devices, per_device(): lax.all_to_all(outgoing, 'fsdp', split_axis=0, concat_axis=0, tiled=True)  7.74 us
  transfers between devices with their start and end apart: 6, of which 4 were waited for; matrix products, arithmetic and copies ran while one was open for 9% of the time, Pallas kernels for 0%

profile of v1, /device:TPU:6, one launch (start us, length us, event | category | flops | bytes accessed | tf_op | source)
XLA Modules:
  0.0 321.9 jit_solution(16638646663496316821)
XLA Ops:
  6.5 0.0 copy-start
  6.5 1.0 constant_dynamic-update-slice_fusion.15
  7.5 0.9 constant_dynamic-update-slice_fusion.14
  8.4 0.9 constant_dynamic-update-slice_fusion.13
  9.2 0.9 constant_dynamic-update-slice_fusion.12
  10.1 0.9 constant_dynamic-update-slice_fusion.11
  10.9 0.9 constant_dynamic-update-slice_fusion.10
  11.8 0.9 constant_dynamic-update-slice_fusion.9
  12.7 0.9 constant_dynamic-update-slice_fusion.8
  13.5 0.9 constant_dynamic-update-slice_fusion.7
  14.4 0.9 constant_dynamic-update-slice_fusion.6
  15.2 0.9 constant_dynamic-update-slice_fusion.5
  16.1 0.9 constant_dynamic-update-slice_fusion.4
  16.9 0.9 constant_dynamic-update-slice_fusion.3
  17.8 0.9 constant_dynamic-update-slice_fusion.2
  18.6 0.9 constant_dynamic-update-slice_fusion.1
  19.5 0.9 constant_dynamic-update-slice_fusion
  20.3 0.0 copy-start.1
  20.4 1.0 copy-done.1
  21.3 0.0 copy-start.3
  21.3 10.6 %all-to-all-start = ((bf16[16,256,128]{2,1,0:T(8,128)(2,1)}), bf16[16,256,128]{2,1,0:T(8,128)(2,1)S(1)}, u32[]{:S(2)}, u32[]{:S(2)}) async-start(bf16[16,256,128]{2,1,0:T(8,128)(2,1)} %bitcast.66), calls=%async_computation | async-start | bytes 2097152 | tf_op jit(solution)/shard_map/all_to_all | solution.py:11
  31.9 0.0 all-gather.4.cloned.1.call-start
  31.9 0.7 all-gather.4.cloned.1.call-update
  32.6 0.0 all-gather.6.cloned.1.call-start
  32.7 26.5 %all-to-all-done = bf16[16,256,128]{2,1,0:T(8,128)(2,1)S(1)} async-done(((bf16[16,256,128]{2,1,0:T(8,128)(2,1)}), bf16[16,256,128]{2,1,0:T(8,128)(2,1)S(1)}, u32[]{:S(2)}, u32[]{:S(2)}) %all-to-all-start) | async-done | bytes 1048608 | tf_op jit(solution)/shard_map/all_to_all | solution.py:11
  59.1 0.0 copy-done
  59.1 0.8 fusion.10
  60.0 20.0 %all-gather.4.cloned.1.call-done = bf16[4096,128]{1,0:T(8,128)(2,1)} async-done(((bf16[256,128]{1,0:T(8,128)(2,1)}), bf16[4096,128]{1,0:T(8,128)(2,1)}) %all-gather.4.cloned.1.call-update) | async-done | bytes 1048592 | tf_op jit(solution)/shard_map/all_gather | solution.py:44
  80.0 2.0 convolution_convert_fusion.1
  82.1 0.7 pad_maximum_fusion.2
  82.7 0.0 all-gather.6.cloned.1.call-update
  82.7 0.0 all-gather.8.cloned.1.call-start
  82.8 0.7 all-gather.8.cloned.1.call-update
  83.5 0.0 copy-done.3
  83.5 0.1 constant_dynamic-slice_fusion
  83.6 0.1 copy.15
  83.7 0.1 reshape.213
  83.8 0.1 copy.27
  83.9 0.1 copy.17
  84.0 0.1 copy.18
  84.1 86.0 %all-gather.6.cloned.1.call-done = bf16[8192,256]{0,1:T(8,128)(2,1)} async-done(((bf16[256,256]{0,1:T(8,128)(2,1)}), bf16[8192,256]{0,1:T(8,128)(2,1)}) %all-gather.6.cloned.1.call-update) | async-done | bytes 4194320 | tf_op jit(solution)/shard_map/all_gather | solution.py:53
  170.2 6.4 %copy.28 = bf16[8192,256]{1,0:T(8,128)(2,1)} copy(bf16[8192,256]{0,1:T(8,128)(2,1)} %all-gather.6.cloned.1.call-done) | data formatting | bytes 8388608 | tf_op jit(solution)/shard_map/reshape | solution.py:53
  176.6 5.0 %gather_fusion = bf16[32,256,256]{2,1,0:T(8,128)(2,1)} fusion(bf16[32,256,256]{2,1,0:T(8,128)(2,1)} %bitcast.63, s32[1024]{0:T(1024)S(1)} %pad_clamp_fusion), kind=kCustom, calls=%fused_computation | custom fusion | bytes 8388736 | tf_op jit(solution)/shard_map/jit(_take)/gather | solution.py:66
  181.5 6.4 %copy.20 = bf16[16,2,256,256]{2,3,1,0:T(8,128)(2,1)} copy(bf16[16,2,256,256]{3,2,1,0:T(8,128)(2,1)} %bitcast.64) | data formatting | bytes 8388608 | tf_op jit(solution)/shard_map/jit(_take)/gather | solution.py:66
  187.9 4.7 %select_select_fusion = bf16[16,2,256,256]{2,3,1,0:T(8,128)(2,1)} fusion(bf16[16,2,256,256]{2,3,1,0:T(8,128)(2,1)} %copy.20, pred[16,2]{1,0:T(8,128)(4,1)S(1)} %copy.18, pred[16,2]{1,0:T(8,128)(4,1)S(1)} %copy.17), kind=kLoop, calls=%fused_computation.6 | loop fusion | flops 4194304 | bytes 8388672 | tf_op jit(solution)/shard_map/jit(_where)/select_n | solution.py:68
  192.6 0.0 copy-start.2
  192.6 7.7 %all-to-all-start.1 = ((bf16[16,2,256,256]{2,3,1,0:T(8,128)(2,1)}), bf16[16,2,256,256]{2,3,1,0:T(8,128)(2,1)}, u32[]{:S(2)}, u32[]{:S(2)}) async-start(bf16[16,2,256,256]{2,3,1,0:T(8,128)(2,1)} %select_select_fusion), calls=%async_computation.1 | async-start | bytes 8388608 | tf_op jit(solution)/shard_map/all_to_all | solution.py:69
  200.4 0.1 constant_dynamic-slice_fusion.1
  200.5 0.6 fusion.45
  203.7 0.1 fusion.17
  203.8 0.0 copy-done.2
  203.8 2.3 collective-permute-start
  206.1 1.4 add_add_fusion
  211.4 92.5 %collective-permute-done = bf16[256,256]{0,1:T(8,128)(2,1)S(1)} collective-permute-done((bf16[256,256]{0,1:T(8,128)(2,1)S(1)}, bf16[256,256]{0,1:T(8,128)(2,1)S(1)}, u32[]{:S(2)}, u32[]{:S(2)}) %collective-permute-start) | collective-permute-done | bytes 131104 | tf_op jit(solution)/shard_map/ppermute | solution.py:17
  304.0 0.0 all-gather.8.cloned.1.call-done
  304.0 3.4 %fusion.9 = bf16[32,4,8,128]{3,2,1,0:T(8,128)(2,1)S(1)} fusion(bf16[256,4096]{1,0:T(8,128)(2,1)S(1)} %copy-done, bf16[4096,512]{1,0:T(8,128)(2,1)} %all-gather.8.cloned.1.call-done), kind=kOutput, calls=%fused_computation.12 | convolution fusion | flops 1073872896 | bytes 6553600 | tf_op jit(solution)/shard_map/dot_general | solution.py:23
  307.4 0.0 all-to-all-done.1
  307.5 2.7 fusion.43
  310.2 1.2 fusion.2
  311.4 1.3 fusion
  312.7 1.8 fusion.14
  314.5 0.8 copy.24
  (16 shorter events, 0.2 us)
Async XLA Ops:
  6.5 52.6 %copy-start = (bf16[256,4096]{1,0:T(8,128)(2,1)S(1)}, bf16[256,4096]{1,0:T(8,128)(2,1)}, u32[]{:S(2)}) copy-start(bf16[256,4096]{1,0:T(8,128)(2,1)} %param.5) | copy-start | bytes 6291460
  20.3 1.0 copy-start.1
  21.3 62.2 %copy-start.3 = (s32[256,2]{0,1:T(2,128)S(1)}, s32[256,2]{0,1:T(2,128)}, u32[]{:S(2)}) copy-start(s32[256,2]{0,1:T(2,128)} %param.9) | copy-start | bytes 6148
  21.3 37.8 %all-to-all-start = ((bf16[16,256,128]{2,1,0:T(8,128)(2,1)}), bf16[16,256,128]{2,1,0:T(8,128)(2,1)S(1)}, u32[]{:S(2)}, u32[]{:S(2)}) async-start(bf16[16,256,128]{2,1,0:T(8,128)(2,1)} %bitcast.66), calls=%async_computation | async-start | bytes 2097152 | tf_op jit(solution)/shard_map/all_to_all | solution.py:11
  31.9 48.1 %all-gather.4.cloned.1.call-start = ((), (), s32[]{:S(2)}) async-start(), calls=%async_computation.2 | async-start | bytes 1114112 | tf_op jit(solution)/shard_map/all_gather | solution.py:44
  32.6 137.5 %all-gather.6.cloned.1.call-start = ((), (), s32[]{:S(2)}) async-start(), calls=%async_computation.3 | async-start | bytes 4325376 | tf_op jit(solution)/shard_map/all_gather | solution.py:53
  82.7 221.3 %all-gather.8.cloned.1.call-start = ((), (), s32[]{:S(2)}) async-start(), calls=%async_computation.4 | async-start | bytes 4456448 | tf_op jit(solution)/shard_map/all_gather | solution.py:42
  192.6 11.2 %copy-start.2 = (bf16[256,256]{0,1:T(8,128)(2,1)S(1)}, bf16[256,256]{0,1:T(8,128)(2,1)}, u32[]{:S(2)}) copy-start(bf16[256,256]{0,1:T(8,128)(2,1)} %pad_maximum_fusion.2) | copy-start | bytes 393220
  192.6 114.8 %all-to-all-start.1 = ((bf16[16,2,256,256]{2,3,1,0:T(8,128)(2,1)}), bf16[16,2,256,256]{2,3,1,0:T(8,128)(2,1)}, u32[]{:S(2)}, u32[]{:S(2)}) async-start(bf16[16,2,256,256]{2,3,1,0:T(8,128)(2,1)} %select_select_fusion), calls=%async_computation.1 | async-start | bytes 8388608 | tf_op jit(solution)/shard_map/all_to_all | solution.py:69
  203.8 100.1 %collective-permute-start = (bf16[256,256]{0,1:T(8,128)(2,1)S(1)}, bf16[256,256]{0,1:T(8,128)(2,1)S(1)}, u32[]{:S(2)}, u32[]{:S(2)}) collective-permute-start(bf16[256,256]{0,1:T(8,128)(2,1)S(1)} %copy-done.2), channel_id=1, source_target_pairs={{0,1},{1,2},{2,3},{3,4},{4,5},{5,6},{6,7},{7,8},{8,9},{9,10},{10,1... | collective-permute-start | bytes 393224 | tf_op jit(solution)/shard_map/ppermute | solution.py:17
Sparse Core Ops, SparseCore 0:
  34.8 45.1 all-gather.3
  83.0 87.0 all-gather.5
  172.3 80.2 all-gather.7
